TPU v7x, 256 devices: a whole 4x4x8 slice. The times are simulated.
256 devices in a mesh: layer: 32 (over z, y), plane: 8 (over x, core).
Axes of the slice: x: 4, y: 4, z: 8, core: 2. Of those that a mesh axis runs over, the one named last changes fastest.
Arguments:
- rhs_field: float32 [32, 2, 4, 64, 1024], P('layer', None, None, None, 'plane'), may hold values from -6 to 6
- panel_inverse: bfloat16 [32, 1024, 2048], P('layer'), may hold values from -1 to 1
- coupling: float32 [32, 2, 4, 64], P('layer', None, None, 'plane'), may hold values from -0.98 to 0.98, as said below
Outputs:
- sweep_field: float32 [32, 2, 4, 64, 1024], P('layer', None, None, None, 'plane')
Inputs may be any that keep to these rules, and one draw needn't show every extreme that they name: Every complex coupling has modulus at most 0.98.
All inputs are finite; a program needn't handle non-finite values.
Results may differ from a plain program's by a relative error of at most 0.025.
Values may be sent and summed in bfloat16 or wider, within the bound.
No kernel may reach another device: no remote copies, remote signals or barrier semaphores. Data moves between devices by JAX's collectives and lax.ppermute only.
A program may use at most 64 MiB of HBM per device.

v0:
```python
import jax
import jax.numpy as jnp
from jax import lax
from jax.sharding import PartitionSpec as P


def complex_product(rows, inverse, width):
    flat = rows.reshape(-1, width)
    product = jnp.dot(flat, inverse, preferred_element_type=jnp.float32)
    product = product.reshape(rows.shape[:-1] + (2 * width,))
    real = product[0, ..., :width] - product[1, ..., width:]
    imag = product[0, ..., width:] + product[1, ..., :width]
    return jnp.stack([real, imag])


def twist(factor, field):
    real = factor[0] * field[0] - factor[1] * field[1]
    imag = factor[0] * field[1] + factor[1] * field[0]
    return jnp.stack([real, imag])


def body(rhs_field, panel_inverse, coupling):
    lines = lax.all_to_all(rhs_field, "plane", split_axis=3, concat_axis=4, tiled=True)[0]
    inverse = panel_inverse[0]
    factors = coupling[0][..., None]
    width = inverse.shape[0]
    layers = lax.axis_size("layer")
    planes = lax.axis_size("plane")
    place = lax.axis_index("layer")
    plane = lax.axis_index("plane")
    pairs = layers // 2
    down = [(2 * j + 1, 2 * j) for j in range(pairs)]
    ahead = [(2 * j, 2 * j + 2) for j in range(pairs - 1)]
    behind = [(2 * j + 2, 2 * j) for j in range(pairs - 1)]
    back = [(2 * j, 2 * j + 1) for j in range(pairs)]
    rows = width // planes
    piece = lax.dynamic_slice_in_dim(inverse, plane * rows, rows, 0)
    piece = lax.ppermute(piece, "layer", down)
    inverse_next = lax.all_gather(piece, "plane", axis=0, tiled=True)
    lines_next = lax.ppermute(lines, "layer", down)
    factors_next = lax.ppermute(factors, "layer", down)

    def pair_forward(incoming):
        mixed = (lines + twist(factors, incoming.astype(jnp.float32))).astype(jnp.bfloat16)
        first = complex_product(mixed, inverse, width)
        carried = first.astype(jnp.bfloat16).astype(jnp.float32)
        mixed = (lines_next + twist(factors_next, carried)).astype(jnp.bfloat16)
        second = complex_product(mixed, inverse_next, width)
        return (first, second)

    first, second = pair_forward(jnp.zeros(lines.shape, jnp.bfloat16))
    valid = place == 0
    store_a = jnp.where(valid, first, 0.0)
    store_b = jnp.where(valid, second, 0.0)

    def forward(section, carry):
        store_a, store_b, outgoing = carry
        incoming = lax.ppermute(outgoing, "layer", ahead)
        first, second = pair_forward(incoming)
        valid = place == 2 * section
        store_a = jnp.where(valid, first, store_a)
        store_b = jnp.where(valid, second, store_b)
        return (store_a, store_b, second.astype(jnp.bfloat16))

    store_a, store_b, _ = lax.fori_loop(
        1, pairs, forward, (store_a, store_b, second.astype(jnp.bfloat16))
    )

    def pair_backward(sweep_b):
        carried = twist(factors_next, sweep_b).astype(jnp.bfloat16)
        sweep_a = store_a + complex_product(carried, inverse, width)
        return (sweep_a, twist(factors, sweep_a).astype(jnp.bfloat16))

    sweep_b = store_b
    sweep_a, outgoing = pair_backward(sweep_b)
    valid = place == layers - 2
    result_a = jnp.where(valid, sweep_a, 0.0)
    result_b = jnp.where(valid, sweep_b, 0.0)

    def backward(section, carry):
        result_a, result_b, outgoing = carry
        incoming = lax.ppermute(outgoing, "layer", behind)
        sweep_b = store_b + complex_product(incoming, inverse_next, width)
        sweep_a, outgoing = pair_backward(sweep_b)
        valid = place == layers - 2 - 2 * section
        result_a = jnp.where(valid, sweep_a, result_a)
        result_b = jnp.where(valid, sweep_b, result_b)
        return (result_a, result_b, outgoing)

    result_a, result_b, _ = lax.fori_loop(1, pairs, backward, (result_a, result_b, outgoing))
    returned = lax.ppermute(result_b, "layer", back)
    result = jnp.where(place % 2 == 0, result_a, returned)
    return lax.all_to_all(result[None], "plane", split_axis=4, concat_axis=3, tiled=True)


def solution(mesh):
    in_specs = (
        P("layer", None, None, None, "plane"),
        P("layer", None, None),
        P("layer", None, None, "plane"),
    )
    out_specs = P("layer", None, None, None, "plane")
    return jax.shard_map(body, mesh=mesh, in_specs=in_specs, out_specs=out_specs, check_vma=False)
```

profile of v0, /device:TPU:120, one launch (start us, length us, event | category | flops | bytes accessed | tf_op | source)
XLA Modules:
  0.0 568.8 jit_solution(8651485035003527377)
XLA Ops:
  10.3 11.1 %collective-permute-done.4 = bf16[128,2048]{1,0:T(8,128)(2,1)S(1)} collective-permute-done((bf16[128,2048]{1,0:T(8,128)(2,1)S(1)}, bf16[128,2048]{1,0:T(8,128)(2,1)S(1)}, u32[]{:S(2)}, u32[]{:S(2)}) %collective-permute-start.4) | collective-permute-done | bytes 524320 | tf_op jit(solution)/shard_map/ppermute | solution.py:38
  24.1 4.3 all-to-all-start
  28.4 4.4 collective-permute-start.3
  36.0 4.4 collective-permute-start.2
  45.5 14.8 %all-gather.2.cloned.1.call-done = bf16[1024,2048]{1,0:T(8,128)(2,1)} async-done(((bf16[128,2048]{1,0:T(8,128)(2,1)}), bf16[1024,2048]{1,0:T(8,128)(2,1)}) %all-gather.2.cloned.1.call-update) | async-done | bytes 4194320 | tf_op jit(solution)/shard_map/all_gather | solution.py:39
  63.5 80.7 %while.34 = (s32[]{:T(128)}, f32[2,4,8,1024]{3,2,1,0:T(8,128)S(1)}, f32[2,4,8,1024]{3,2,1,0:T(8,128)S(1)}, bf16[2,4,8,1024]{3,2,1,0:T(8,128)(2,1)S(1)}, s32[]{:T...) while((s32[]{:T(128)}, f32[2,4,8,1024]{3,2,1,0:T(8,128)S(1)}, ...), condition=%wide.region_1.2_spmd, body=%wide.region_0.1_spmd.sunk | while | flops 538312704 | bytes 33294036 | solution.py:65
  64.3 3.2 fusion.65
  69.7 3.2 fusion.65
  75.1 3.2 fusion.65
  80.5 3.2 fusion.65
  85.9 3.2 fusion.65
  96.6 3.2 fusion.65
  102.0 3.2 fusion.65
  112.8 3.2 fusion.65
  118.2 3.2 fusion.65
  123.5 3.2 fusion.65
  128.9 3.2 fusion.65
  134.3 3.2 fusion.65
  147.6 80.6 %while.35 = (s32[]{:T(128)}, f32[2,4,8,1024]{3,2,1,0:T(8,128)S(1)}, f32[2,4,8,1024]{3,2,1,0:T(8,128)S(1)}, bf16[2,4,8,1024]{3,2,1,0:T(8,128)(2,1)S(1)}, s32[]{:T...) while((s32[]{:T(128)}, f32[2,4,8,1024]{3,2,1,0:T(8,128)S(1)}, ...), condition=%wide.region_3.4_spmd, body=%wide.region_2.3_spmd.sunk | while | flops 538050560 | bytes 32245480 | solution.py:90
  229.5 299.4 %collective-permute-done.5 = f32[2,4,8,1024]{3,2,1,0:T(8,128)S(1)} collective-permute-done((f32[2,4,8,1024]{3,2,1,0:T(8,128)S(1)}, f32[2,4,8,1024]{3,2,1,0:T(8,128)S(1)}, u32[]{:S(2)}, u32[]{:S(2)}) %collective-permute-start.5) | collective-permute-done | bytes 262176 | tf_op jit(solution)/shard_map/ppermute | solution.py:91
  532.0 6.5 %reshape.75 = f32[8,1,8192]{2,1,0:T(1,128)S(1)} reshape(f32[1024,1,2,4,8]{4,3,2,1,0:T(4,128)} %bitcast.114) | data formatting | bytes 524288
  538.6 10.3 %all_to_all.33 = f32[8,1,8192]{2,1,0:T(1,128)S(1)} all-to-all(f32[8,1,8192]{2,1,0:T(1,128)S(1)} %reshape.75), channel_id=1, replica_groups=mesh['layer'=32,'plane'=8] {'plane'}, dimensions={0} | all-to-all | bytes 524288 | tf_op jit(solution)/shard_map/all_to_all | solution.py:93
  550.6 6.9 %reshape.76 = f32[1024,1,2,4,8]{4,3,2,1,0:T(4,128)} reshape(f32[8,8192]{1,0:T(8,128)S(1)} %reduce) | data formatting | bytes 524288
  557.5 4.4 copy.24
  (476 shorter events, 146.7 us)
Async XLA Ops:
  6.5 53.8 %all-gather.2.cloned.1.call-start = ((), (), s32[]{:S(2)}) async-start(), calls=%async_computation.2 | async-start | bytes 4718592 | tf_op jit(solution)/shard_map/all_gather | solution.py:39
  7.6 13.8 %collective-permute-start.4 = (bf16[128,2048]{1,0:T(8,128)(2,1)S(1)}, bf16[128,2048]{1,0:T(8,128)(2,1)S(1)}, u32[]{:S(2)}, u32[]{:S(2)}) collective-permute-start(bf16[128,2048]{1,0:T(8,128)(2,1)S(1)} %dynamic-slice_bitcast_fusion), channel_id=1, source_target_pairs={{8,0},{24,16},{40,32},{56,48},{72,64},{88,80},{104,96},{120,112},{... | collective-permute-start | bytes 1572872 | tf_op jit(solution)/shard_map/ppermute | solution.py:38
  24.1 11.8 %all-to-all-start = ((f32[1,2,4,64,128]{4,2,1,0,3:T(4,128)}), f32[1,2,4,64,128]{4,2,1,0,3:T(4,128)S(1)}, u32[]{:S(2)}, u32[]{:S(2)}) async-start(f32[1,2,4,64,128]{4,2,1,0,3:T(4,128)} %copy.17), calls=%async_computation | async-start | bytes 524288 | tf_op jit(solution)/shard_map/all_to_all | solution.py:23
  28.4 5.9 %collective-permute-start.3 = (f32[2,4,8,1]{2,1,0,3:T(4,128)}, f32[2,4,8,1]{2,1,0,3:T(4,128)S(1)}, u32[]{:S(2)}, u32[]{:S(2)}) collective-permute-start(f32[2,4,8,1]{2,1,0,3:T(4,128)} %bitcast.120), channel_id=1, source_target_pairs={{8,0},{24,16},{40,32},{56,48},{72,64},{88,80},{104,96},{120,112},{... | collective-permute-start | bytes 776 | tf_op jit(solution)/shard_map/ppermute | solution.py:41
  36.0 9.6 %collective-permute-start.2 = (f32[2,4,8,1024]{3,2,1,0:T(8,128)S(1)}, f32[2,4,8,1024]{3,2,1,0:T(8,128)S(1)}, u32[]{:S(2)}, u32[]{:S(2)}) collective-permute-start(f32[2,4,8,1024]{3,2,1,0:T(8,128)S(1)} %bitcast.116), channel_id=1, source_target_pairs={{8,0},{24,16},{40,32},{56,48},{72,64},{88,80},{104,96},{120,112},{... | collective-permute-start | bytes 786440 | tf_op jit(solution)/shard_map/ppermute | solution.py:40
  63.5 0.7 collective-permute-start
  68.9 0.7 collective-permute-start
  74.2 0.7 collective-permute-start
  79.6 0.7 collective-permute-start
  85.0 0.7 collective-permute-start
  90.4 0.7 collective-permute-start
  95.8 0.7 collective-permute-start
  101.2 0.7 collective-permute-start
  106.5 0.7 collective-permute-start
  111.9 0.7 collective-permute-start
  117.3 0.7 collective-permute-start
  122.7 0.7 collective-permute-start
  128.1 0.7 collective-permute-start
  133.4 0.7 collective-permute-start
  138.8 0.7 collective-permute-start
  147.6 0.7 collective-permute-start.1
  158.4 0.7 collective-permute-start.1
  163.7 0.7 collective-permute-start.1
  228.2 300.8 %collective-permute-start.5 = (f32[2,4,8,1024]{3,2,1,0:T(8,128)S(1)}, f32[2,4,8,1024]{3,2,1,0:T(8,128)S(1)}, u32[]{:S(2)}, u32[]{:S(2)}) collective-permute-start(f32[2,4,8,1024]{3,2,1,0:T(8,128)S(1)} %get-tuple-element.378), channel_id=1, source_target_pairs={{0,8},{16,24},{32,40},{48,56},{64,72},{80,88},{96,104},{112,120},{... | collective-permute-start | bytes 786440 | tf_op jit(solution)/shard_map/ppermute | solution.py:91
  (44 other events, 133.1 us)
Sparse Core Ops, SparseCore 0:
  22.4 37.9 all-gather.1
where the time goes:
time: 570 us; the launch traced here: 569 us
  waiting for transfers between devices  329 us (58%)
  matrix products  130 us (23%)
  starting transfers between devices  37.1 us (7%)
  local copies, waits for them, and re-layouts  27.3 us (5%)
  other arithmetic  17.9 us (3%)
  between operations  13.6 us (2%)
  blocking collectives  10.3 us (2%)
    ppermute x1, waiting for transfers between devices, body(): returned = lax.ppermute(result_b, 'layer', back)  299 us
    dot_general x63, matrix products, complex_product(): product = jnp.dot(flat, inverse, preferred_element_type=jnp.float32)  130 us
    unnamed x7, local copies, waits for them, and re-layouts  16.1 us
    all_gather x1, waiting for transfers between devices, body(): inverse_next = lax.all_gather(piece, 'plane', axis=0, tiled=True)  14.8 us
  transfers between devices with their start and end apart: 36, of which 6 were waited for; matrix products, arithmetic and copies ran while one was open for 1% of the time, Pallas kernels for 0%

commit v1 on v0

--- a/solution.py
+++ b/solution.py
@@ -90,7 +90,12 @@
     result_a, result_b, _ = lax.fori_loop(1, pairs, backward, (result_a, result_b, outgoing))
     returned = lax.ppermute(result_b, "layer", back)
     result = jnp.where(place % 2 == 0, result_a, returned)
-    return lax.all_to_all(result[None], "plane", split_axis=4, concat_axis=3, tiled=True)
+    return jnp.concatenate(
+        lax.all_to_all(
+            jnp.stack(jnp.split(result[None], lax.axis_size("plane"), axis=4)), "plane", 0, 0
+        ),
+        axis=3,
+    )
 
 
 def solution(mesh):

time: 570 us -> 548 us (0.961)
  local copies, waits for them, and re-layouts: 27.3 us -> 6.62 us
    unnamed x7 -> x12, local copies, waits for them, and re-layouts: 16.1 us -> 2.67 us
where the time goes in v1:
time: 548 us; the launch traced here: 547 us
  waiting for transfers between devices  329 us (60%)
  matrix products  130 us (24%)
  starting transfers between devices  37.1 us (7%)
  other arithmetic  16.7 us (3%)
  between operations  13.6 us (2%)
  blocking collectives  10.2 us (2%)
  local copies, waits for them, and re-layouts  6.62 us (1%)
    ppermute x1, waiting for transfers between devices, body(): returned = lax.ppermute(result_b, 'layer', back)  299 us
    dot_general x63, matrix products, complex_product(): product = jnp.dot(flat, inverse, preferred_element_type=jnp.float32)  130 us
    all_gather x1, waiting for transfers between devices, body(): inverse_next = lax.all_gather(piece, 'plane', axis=0, tiled=True)  14.8 us
    ppermute x1, waiting for transfers between devices, body(): piece = lax.ppermute(piece, 'layer', down)  11.1 us
  transfers between devices with their start and end apart: 36, of which 6 were waited for; matrix products, arithmetic and copies ran while one was open for 1% of the time, Pallas kernels for 0%

profile of v1, /device:TPU:120, one launch (start us, length us, event | category | flops | bytes accessed | tf_op | source)
XLA Modules:
  0.0 546.9 jit_solution(14924563763086433845)
XLA Ops:
  10.3 11.1 %collective-permute-done.4 = bf16[128,2048]{1,0:T(8,128)(2,1)S(1)} collective-permute-done((bf16[128,2048]{1,0:T(8,128)(2,1)S(1)}, bf16[128,2048]{1,0:T(8,128)(2,1)S(1)}, u32[]{:S(2)}, u32[]{:S(2)}) %collective-permute-start.4) | collective-permute-done | bytes 524320 | tf_op jit(solution)/shard_map/ppermute | solution.py:38
  24.1 4.3 all-to-all-start
  28.4 4.4 collective-permute-start.3
  35.9 4.4 collective-permute-start.2
  45.5 14.8 %all-gather.2.cloned.1.call-done = bf16[1024,2048]{1,0:T(8,128)(2,1)} async-done(((bf16[128,2048]{1,0:T(8,128)(2,1)}), bf16[1024,2048]{1,0:T(8,128)(2,1)}) %all-gather.2.cloned.1.call-update) | async-done | bytes 4194320 | tf_op jit(solution)/shard_map/all_gather | solution.py:39
  63.5 80.7 %while.34 = (s32[]{:T(128)}, f32[2,4,8,1024]{3,2,1,0:T(8,128)S(1)}, f32[2,4,8,1024]{3,2,1,0:T(8,128)S(1)}, bf16[2,4,8,1024]{3,2,1,0:T(8,128)(2,1)S(1)}, s32[]{:T...) while((s32[]{:T(128)}, f32[2,4,8,1024]{3,2,1,0:T(8,128)S(1)}, ...), condition=%wide.region_1.2_spmd, body=%wide.region_0.1_spmd.sunk | while | flops 538312704 | bytes 33294036 | solution.py:65
  64.3 3.2 fusion.74
  69.7 3.2 fusion.74
  75.1 3.2 fusion.74
  80.5 3.2 fusion.74
  85.9 3.2 fusion.74
  91.2 3.2 fusion.74
  96.6 3.2 fusion.74
  102.0 3.2 fusion.74
  107.4 3.2 fusion.74
  112.8 3.2 fusion.74
  118.2 3.2 fusion.74
  123.5 3.2 fusion.74
  128.9 3.2 fusion.74
  134.3 3.2 fusion.74
  139.7 3.2 fusion.74
  147.6 80.6 %while.35 = (s32[]{:T(128)}, f32[2,4,8,1024]{3,2,1,0:T(8,128)S(1)}, f32[2,4,8,1024]{3,2,1,0:T(8,128)S(1)}, bf16[2,4,8,1024]{3,2,1,0:T(8,128)(2,1)S(1)}, s32[]{:T...) while((s32[]{:T(128)}, f32[2,4,8,1024]{3,2,1,0:T(8,128)S(1)}, ...), condition=%wide.region_3.4_spmd, body=%wide.region_2.3_spmd.sunk | while | flops 538050560 | bytes 32245480 | solution.py:90
  229.5 299.4 %collective-permute-done.5 = f32[2,4,8,1024]{3,2,1,0:T(8,128)S(1)} collective-permute-done((f32[2,4,8,1024]{3,2,1,0:T(8,128)S(1)}, f32[2,4,8,1024]{3,2,1,0:T(8,128)S(1)}, u32[]{:S(2)}, u32[]{:S(2)}) %collective-permute-start.5) | collective-permute-done | bytes 262176 | tf_op jit(solution)/shard_map/ppermute | solution.py:91
  529.1 10.2 %all_to_all.20 = f32[8,1,2,4,8,128]{5,4,3,2,1,0:T(8,128)S(1)} all-to-all(f32[8,1,2,4,8,128]{5,4,3,2,1,0:T(8,128)S(1)} %fusion.42), channel_id=1, replica_groups=mesh['layer'=32,'plane'=8] {'plane'}, dimensions={0} | all-to-all | bytes 524288 | tf_op jit(solution)/shard_map/all_to_all | solution.py:94
  (479 shorter events, 133.1 us)
Async XLA Ops:
  6.5 53.8 %all-gather.2.cloned.1.call-start = ((), (), s32[]{:S(2)}) async-start(), calls=%async_computation.2 | async-start | bytes 4718592 | tf_op jit(solution)/shard_map/all_gather | solution.py:39
  7.6 13.8 %collective-permute-start.4 = (bf16[128,2048]{1,0:T(8,128)(2,1)S(1)}, bf16[128,2048]{1,0:T(8,128)(2,1)S(1)}, u32[]{:S(2)}, u32[]{:S(2)}) collective-permute-start(bf16[128,2048]{1,0:T(8,128)(2,1)S(1)} %dynamic-slice_bitcast_fusion), channel_id=1, source_target_pairs={{8,0},{24,16},{40,32},{56,48},{72,64},{88,80},{104,96},{120,112},{... | collective-permute-start | bytes 1572872 | tf_op jit(solution)/shard_map/ppermute | solution.py:38
  24.1 11.8 %all-to-all-start = ((f32[1,2,4,64,128]{4,2,1,0,3:T(4,128)}), f32[1,2,4,64,128]{4,2,1,0,3:T(4,128)S(1)}, u32[]{:S(2)}, u32[]{:S(2)}) async-start(f32[1,2,4,64,128]{4,2,1,0,3:T(4,128)} %copy.9), calls=%async_computation | async-start | bytes 524288 | tf_op jit(solution)/shard_map/all_to_all | solution.py:23
  28.4 5.9 %collective-permute-start.3 = (f32[2,4,8,1]{2,1,0,3:T(4,128)}, f32[2,4,8,1]{2,1,0,3:T(4,128)S(1)}, u32[]{:S(2)}, u32[]{:S(2)}) collective-permute-start(f32[2,4,8,1]{2,1,0,3:T(4,128)} %bitcast.149), channel_id=1, source_target_pairs={{8,0},{24,16},{40,32},{56,48},{72,64},{88,80},{104,96},{120,112},{... | collective-permute-start | bytes 776 | tf_op jit(solution)/shard_map/ppermute | solution.py:41
  35.9 9.6 %collective-permute-start.2 = (f32[2,4,8,1024]{3,2,1,0:T(8,128)S(1)}, f32[2,4,8,1024]{3,2,1,0:T(8,128)S(1)}, u32[]{:S(2)}, u32[]{:S(2)}) collective-permute-start(f32[2,4,8,1024]{3,2,1,0:T(8,128)S(1)} %bitcast.145), channel_id=1, source_target_pairs={{8,0},{24,16},{40,32},{56,48},{72,64},{88,80},{104,96},{120,112},{... | collective-permute-start | bytes 786440 | tf_op jit(solution)/shard_map/ppermute | solution.py:40
  63.5 0.7 collective-permute-start
  68.9 0.7 collective-permute-start
  74.2 0.7 collective-permute-start
  79.6 0.7 collective-permute-start
  85.0 0.7 collective-permute-start
  90.4 0.7 collective-permute-start
  95.8 0.7 collective-permute-start
  101.1 0.7 collective-permute-start
  106.5 0.7 collective-permute-start
  111.9 0.7 collective-permute-start
  117.3 0.7 collective-permute-start
  122.7 0.7 collective-permute-start
  128.1 0.7 collective-permute-start
  133.4 0.7 collective-permute-start
  138.8 0.7 collective-permute-start
  147.6 0.7 collective-permute-start.1
  153.0 0.7 collective-permute-start.1
  158.3 0.7 collective-permute-start.1
  228.2 300.8 %collective-permute-start.5 = (f32[2,4,8,1024]{3,2,1,0:T(8,128)S(1)}, f32[2,4,8,1024]{3,2,1,0:T(8,128)S(1)}, u32[]{:S(2)}, u32[]{:S(2)}) collective-permute-start(f32[2,4,8,1024]{3,2,1,0:T(8,128)S(1)} %get-tuple-element.378), channel_id=1, source_target_pairs={{0,8},{16,24},{32,40},{48,56},{64,72},{80,88},{96,104},{112,120},{... | collective-permute-start | bytes 786440 | tf_op jit(solution)/shard_map/ppermute | solution.py:91
  (44 other events, 133.1 us)
Sparse Core Ops, SparseCore 0:
  22.4 37.9 all-gather.1
